TPU v7x, 128 devices: a whole 4x4x4 slice. The times are simulated.
128 devices in a mesh: dp: 32 (over z, y, core), mp: 4 (over x).
Axes of the slice: x: 4, y: 4, z: 4, core: 2. Of those that a mesh axis runs over, the one named last changes fastest.
Arguments:
- tokens: bfloat16 [57344, 1024], P('dp'), may hold values from -60 to 60
- segment_ids: int32 [57344], P('dp'), may hold values from 0 to 127, as said below
- page_table: int32 [448], P('dp'), may hold values from 0 to 447, as said below
- w_query: bfloat16 [1024, 1024], P('dp', 'mp'), may hold values from -0.1875 to 0.1875
- w_key: bfloat16 [1024, 1024], P('dp', 'mp'), may hold values from -0.1875 to 0.1875
- w_value: bfloat16 [1024, 1024], P('dp', 'mp'), may hold values from -0.1875 to 0.1875
- w_out: bfloat16 [1024, 1024], P('mp', 'dp'), may hold values from -1.5 to 1.5
- w_up: bfloat16 [1024, 4096], P('dp', 'mp'), may hold values from -0.1875 to 0.1875
- w_down: bfloat16 [4096, 1024], P('mp', 'dp'), may hold values from -0.09375 to 0.09375
- gain_first: float32 [1024], replicated, may hold values from 0.1 to 1.9
- shift_first: float32 [1024], replicated, may hold values from -3 to 3
- gain_second: float32 [1024], replicated, may hold values from 0.1 to 1.9
- shift_second: float32 [1024], replicated, may hold values from -3 to 3
Outputs:
- mixed: bfloat16 [57344, 1024], P('dp')
- kv_cache: bfloat16 [57344, 2, 1024], P('dp', None, 'mp')
Inputs may be any that keep to these rules, and one draw needn't show every extreme that they name: page_table is a permutation of the page slots. Page p lies on device p // 14 in arrival order and goes to device page_table[p] // 14; from one device at most 1 pages go to one device, and some pair reaches 1. `segment_ids`: tokens with equal ids form one request; after dealing, a request's tokens are consecutive and lie on one device, which holds at most 4 requests.
All inputs are finite; a program needn't handle non-finite values.
Results may differ from a plain program's by a relative error of at most 0.014.
Values may be sent and summed in bfloat16 or wider, within the bound.
No kernel may reach another device: no remote copies, remote signals or barrier semaphores. Data moves between devices by JAX's collectives and lax.ppermute only.
A program may use at most 128 MiB of HBM per device.

v0:
```python
import jax
import jax.numpy as jnp
from jax import lax
from jax.sharding import PartitionSpec as P

HEAD = 64


def layer_norm(hidden_sum, gain, shift):
    center = hidden_sum - jnp.mean(hidden_sum, axis=-1, keepdims=True)
    spread = jnp.mean(center * center, axis=-1, keepdims=True)
    return center * lax.rsqrt(spread + 1e-05) * gain + shift


def attend_head(query, keys, values, segments, block_rows):
    blocks = query.shape[0] // block_rows
    query_blocks = query.reshape(blocks, block_rows, query.shape[1])
    segment_blocks = segments.reshape(blocks, block_rows)

    def per_block(bundle):
        rows, row_ids = bundle
        scores = jnp.einsum("qd,kd->qk", rows, keys, preferred_element_type=jnp.float32) * HEAD ** (
            -0.5
        )
        scores = jnp.where(row_ids[:, None] == segments[None, :], scores, -1e30)
        highest = jnp.max(scores, axis=1, keepdims=True)
        raised = jnp.exp(scores - highest)
        attn_weights = (raised / jnp.sum(raised, axis=1, keepdims=True)).astype(jnp.bfloat16)
        return jnp.dot(attn_weights, values, preferred_element_type=jnp.float32).astype(
            jnp.bfloat16
        )

    return lax.map(per_block, (query_blocks, segment_blocks)).reshape(
        query.shape[0], values.shape[1]
    )


def body(
    tokens,
    segment_ids,
    page_table,
    w_query,
    w_key,
    w_value,
    w_out,
    w_up,
    w_down,
    gain_first,
    shift_first,
    gain_second,
    shift_second,
):
    n_data = lax.axis_size("dp")
    n_model = lax.axis_size("mp")
    me_model = lax.axis_index("mp")
    pages_dev = page_table.shape[0]
    page = tokens.shape[0] // pages_dev
    width = tokens.shape[1]
    quarter = width // n_model
    sub = page // n_model
    slots_per = (pages_dev + n_data - 1) // n_data
    buffer_rows = n_data * slots_per
    head_cols = w_query.shape[1]
    unit_cols = w_up.shape[1]
    local = jnp.concatenate([w_query, w_key, w_value, w_up, w_out.T, w_down.T], axis=1)
    gathered = lax.all_gather(local, "dp", axis=0, tiled=True)
    at = 0
    full_query = gathered[:, at : at + head_cols]
    at += head_cols
    full_key = gathered[:, at : at + head_cols]
    at += head_cols
    full_value = gathered[:, at : at + head_cols]
    at += head_cols
    full_up = gathered[:, at : at + unit_cols]
    at += unit_cols
    out_t = gathered[:, at : at + w_out.shape[0]]
    at += w_out.shape[0]
    down_t = gathered[:, at : at + w_down.shape[0]]
    out_all_t = lax.all_gather(out_t, "mp", axis=1, tiled=True)
    target = page_table // pages_dev
    local_slot = page_table % pages_dev
    order = jnp.arange(pages_dev, dtype=jnp.int32)
    earlier = (target[:, None] == target[None, :]) & (order[:, None] < order[None, :])
    rank = jnp.sum(earlier.astype(jnp.int32), axis=0)
    position = target * slots_per + rank
    meta = jnp.concatenate([segment_ids.reshape(pages_dev, page), local_slot[:, None]], axis=1)
    send_meta = (
        jnp.zeros((buffer_rows, page + 1), jnp.int32).at[:, page].set(-1).at[position].set(meta)
    )
    token_part = lax.dynamic_slice_in_dim(tokens, me_model * quarter, quarter, axis=1)
    send_pages = (
        jnp.zeros((buffer_rows, page, quarter), tokens.dtype)
        .at[position]
        .set(token_part.reshape(pages_dev, page, quarter))
    )
    got_pages = lax.all_to_all(send_pages, "dp", split_axis=0, concat_axis=0, tiled=True)
    got_meta = lax.all_to_all(send_meta, "dp", split_axis=0, concat_axis=0, tiled=True)
    got_ids = got_meta[:, :page]
    got_slots = got_meta[:, page]
    matches = got_slots[None, :] == order[:, None]
    source_row = jnp.sum(
        jnp.where(matches, jnp.arange(buffer_rows, dtype=jnp.int32)[None, :], 0), axis=1
    )
    dealt_part = got_pages[source_row]
    dealt = lax.all_gather(dealt_part, "mp", axis=2, tiled=True).reshape(pages_dev * page, width)
    dealt_ids = got_ids[source_row].reshape(pages_dev * page)
    query = jnp.dot(dealt, full_query, preferred_element_type=jnp.float32).astype(jnp.bfloat16)
    keys = jnp.dot(dealt, full_key, preferred_element_type=jnp.float32).astype(jnp.bfloat16)
    values = jnp.dot(dealt, full_value, preferred_element_type=jnp.float32).astype(jnp.bfloat16)
    suitable = [
        count for count in range(1, pages_dev + 1) if pages_dev % count == 0 and count * page >= 512
    ]
    block_rows = suitable[0] * page
    heads_here = query.shape[1] // HEAD
    contexts = []
    for head in range(heads_here):
        cols = slice(head * HEAD, (head + 1) * HEAD)
        contexts.append(
            attend_head(query[:, cols], keys[:, cols], values[:, cols], dealt_ids, block_rows)
        )
    context = jnp.concatenate(contexts, axis=1)
    context_rows = lax.all_to_all(
        context.reshape(pages_dev, n_model, sub, head_cols),
        "mp",
        split_axis=1,
        concat_axis=1,
        tiled=True,
    )
    attended = jnp.zeros((pages_dev, sub, width), jnp.float32)
    for group in range(n_model):
        term = jnp.einsum(
            "pic,oc->pio",
            context_rows[:, group],
            out_all_t[:, group * head_cols : (group + 1) * head_cols],
            preferred_element_type=jnp.float32,
        ).astype(jnp.bfloat16)
        attended = attended + term.astype(jnp.float32)
    dealt_mine = lax.dynamic_index_in_dim(
        dealt.reshape(pages_dev, n_model, sub, width), me_model, axis=1, keepdims=False
    )
    first_mine = layer_norm(
        dealt_mine.astype(jnp.float32) + attended, gain_first, shift_first
    ).astype(jnp.bfloat16)
    first = lax.all_gather(first_mine, "mp", axis=1).reshape(pages_dev * page, width)
    hidden = jax.nn.gelu(
        jnp.dot(first, full_up, preferred_element_type=jnp.float32), approximate=False
    ).astype(jnp.bfloat16)
    fed_term = jnp.einsum("tu,ou->to", hidden, down_t, preferred_element_type=jnp.float32).astype(
        jnp.bfloat16
    )
    fed = lax.psum_scatter(
        fed_term.reshape(pages_dev, n_model, sub, width), "mp", scatter_dimension=1, tiled=True
    ).reshape(pages_dev, sub, width)
    second_mine = layer_norm(
        first_mine.astype(jnp.float32) + fed.astype(jnp.float32), gain_second, shift_second
    ).astype(jnp.bfloat16)
    valid = got_slots >= 0
    outgoing = jnp.where(
        valid[:, None, None],
        second_mine[jnp.clip(got_slots, 0, pages_dev - 1)],
        jnp.zeros((), second_mine.dtype),
    )
    returned = lax.all_to_all(outgoing, "dp", split_axis=0, concat_axis=0, tiled=True)
    mixed_mine = returned[position]
    mixed = lax.all_gather(mixed_mine, "mp", axis=1).reshape(pages_dev * page, width)
    kv_cache = jnp.stack([keys, values], axis=1)
    return (mixed, kv_cache)


def solution(mesh):
    return jax.shard_map(
        body,
        mesh=mesh,
        in_specs=(
            P("dp", None),
            P("dp"),
            P("dp"),
            P("dp", "mp"),
            P("dp", "mp"),
            P("dp", "mp"),
            P("mp", "dp"),
            P("dp", "mp"),
            P("mp", "dp"),
            P(),
            P(),
            P(),
            P(),
        ),
        out_specs=(P("dp", None), P("dp", None, "mp")),
        check_vma=False,
    )
```

profile of v0, /device:TPU:1, one launch (start us, length us, event | category | flops | bytes accessed | tf_op | source)
XLA Modules:
  0.0 474.3 jit_solution(7659568354544722614)
XLA Ops:
  10.2 9.6 %all-to-all-start = ((s32[32,1,129]{2,1,0:T(1,128)}), s32[32,1,129]{2,1,0:T(1,128)S(1)}, u32[]{:S(2)}, u32[]{:S(2)}) async-start(s32[32,1,129]{2,1,0:T(1,128)} %all_to_all.17), calls=%async_computation | async-start | bytes 65536 | tf_op jit(solution)/shard_map/all_to_all | solution.py:97
  21.1 1.6 broadcast_in_dim.96
  22.7 2.8 scatter_fusion
  25.5 1.5 all-to-all-done
  27.1 5.9 %all-to-all-start.1 = ((bf16[32,128,256]{2,1,0:T(8,128)(2,1)}), bf16[32,128,256]{2,1,0:T(8,128)(2,1)S(1)}, u32[]{:S(2)}, u32[]{:S(2)}) async-start(bf16[32,128,256]{2,1,0:T(8,128)(2,1)} %scatter_fusion), calls=%async_computation.1 | async-start | bytes 4194304 | tf_op jit(solution)/shard_map/all_to_all | solution.py:96
  34.2 27.3 %all-to-all-done.1 = bf16[32,128,256]{2,1,0:T(8,128)(2,1)S(1)} async-done(((bf16[32,128,256]{2,1,0:T(8,128)(2,1)}), bf16[32,128,256]{2,1,0:T(8,128)(2,1)S(1)}, u32[]{:S(2)}, u32[]{:S(2)}) %all-to-all-start.1) | async-done | bytes 2097184 | tf_op jit(solution)/shard_map/all_to_all | solution.py:96
  61.5 1.5 gather_fusion
  64.6 42.6 %all-gather.13.cloned.1.call-done = bf16[14,128,1024]{2,1,0:T(8,128)(2,1)} async-done(((bf16[14,128,256]{2,1,0:T(8,128)(2,1)}), bf16[14,128,1024]{2,1,0:T(8,128)(2,1)}) %all-gather.13.cloned.1.call-update) | async-done | bytes 3670032 | tf_op jit(solution)/shard_map/all_gather | solution.py:105
  107.2 54.7 %all-gather.9.cloned.1.call-done = bf16[1024,3072]{1,0:T(8,128)(2,1)} async-done(((bf16[32,3072]{1,0:T(8,128)(2,1)}), bf16[1024,3072]{1,0:T(8,128)(2,1)}) %all-gather.9.cloned.1.call-update) | async-done | bytes 6291472 | tf_op jit(solution)/shard_map/all_gather | solution.py:66
  162.0 3.3 convolution_convert_fusion.2
  167.2 3.3 convolution_convert_fusion.1
  172.6 3.3 convolution_convert_fusion.3
  176.9 8.2 %while.41 = (s32[]{:T(128)}, bf16[2,896,64]{1,2,0:T(8,128)(2,1)S(1)}, s32[2,896]{1,0:T(2,128)S(1)}, s32[14,128]{1,0:T(8,128)S(1)}, bf16[2,896,64]{2,1,0:T(8,128)...) while((s32[]{:T(128)}, bf16[2,896,64]{1,2,0:T(8,128)(2,1)S(1)}, ...), condition=%wide.region_7.8_spmd, body=%wide.region_4.7_spmd.sunk | while | flops 425548032 | bytes 20567648 | solution.py:33
  179.8 1.5 fusion.137
  183.6 1.5 fusion.137
  187.0 7.7 %while.42 = (s32[]{:T(128)}, bf16[2,896,64]{1,2,0:T(8,128)(2,1)S(1)}, s32[2,896]{1,0:T(2,128)S(1)}, s32[14,128]{1,0:T(8,128)S(1)}, bf16[2,896,64]{2,1,0:T(8,128)...) while((s32[]{:T(128)}, bf16[2,896,64]{1,2,0:T(8,128)(2,1)S(1)}, ...), condition=%wide.region_11.12_spmd, body=%wide.region_8.11_spmd.sunk | while | flops 425548032 | bytes 20567648 | solution.py:33
  189.3 1.5 fusion.142
  193.1 1.5 fusion.142
  195.8 7.8 %while.43 = (s32[]{:T(128)}, bf16[2,896,64]{1,2,0:T(8,128)(2,1)S(1)}, s32[2,896]{1,0:T(2,128)S(1)}, s32[14,128]{1,0:T(8,128)S(1)}, bf16[2,896,64]{2,1,0:T(8,128)...) while((s32[]{:T(128)}, bf16[2,896,64]{1,2,0:T(8,128)(2,1)S(1)}, ...), condition=%wide.region_15.16_spmd, body=%wide.region_12.15_spmd.sunk | while | flops 425548032 | bytes 20567648 | solution.py:33
  198.1 1.5 fusion.147
  201.9 1.5 fusion.147
  204.8 1.9 slice.152
  206.7 7.7 %while.44 = (s32[]{:T(128)}, bf16[2,896,64]{1,2,0:T(8,128)(2,1)S(1)}, s32[2,896]{1,0:T(2,128)S(1)}, s32[14,128]{1,0:T(8,128)S(1)}, bf16[2,896,64]{2,1,0:T(8,128)...) while((s32[]{:T(128)}, bf16[2,896,64]{1,2,0:T(8,128)(2,1)S(1)}, ...), condition=%wide.region_19.20_spmd, body=%wide.region_16.19_spmd.sunk | while | flops 425548032 | bytes 20567648 | solution.py:33
  209.0 1.5 fusion.152
  212.8 1.5 fusion.152
  216.3 4.0 all-to-all-start.2
  220.2 19.1 %all-to-all-done.2 = bf16[14,4,32,256]{3,2,0,1:T(8,128)(2,1)S(1)} async-done(((bf16[14,4,32,256]{3,2,0,1:T(8,128)(2,1)}), bf16[14,4,32,256]{3,2,0,1:T(8,128)(2,1)S(1)}, u32[]{:S(2)}, u32[]{:S(2)}) %all-to-all-start.2) | async-done | bytes 917536 | tf_op jit(solution)/shard_map/all_to_all | solution.py:122
  239.3 6.3 %all-gather.11.cloned.1.call-done = bf16[1024,1024]{1,0:T(8,128)(2,1)} async-done(((bf16[1024,256]{1,0:T(8,128)(2,1)}), bf16[1024,1024]{1,0:T(8,128)(2,1)}) %all-gather.11.cloned.1.call-update) | async-done | bytes 2097168 | tf_op jit(solution)/shard_map/all_gather | solution.py:79
  245.7 1.5 convolution_convert_fusion.7
  247.2 1.5 convolution_convert_fusion.6
  248.6 1.5 convolution_convert_fusion.5
  250.1 2.2 fusion.100
  254.0 44.9 %all-gather.15.cloned.1.call-done = bf16[14,128,1024]{2,1,0:T(8,128)(2,1)} async-done(((bf16[14,32,1024]{2,1,0:T(8,128)(2,1)}), bf16[14,128,1024]{2,1,0:T(8,128)(2,1)}) %all-gather.15.cloned.1.call-update) | async-done | bytes 3670032 | tf_op jit(solution)/shard_map/all_gather | solution.py:144
  298.9 26.1 %convolution_convert_fusion = bf16[1792,1024]{1,0:T(8,128)(2,1)} fusion(bf16[1024,3072]{1,0:T(8,128)(2,1)} %all-gather.9.cloned.1.call-done, bf16[1792,1024]{1,0:T(8,128)(2,1)} %bitcast.184), kind=kOutput, calls=%fused_computation.73 | convolution fusion | flops 7637303296 | bytes 11534336 | tf_op jit(solution)/shard_map/tu,ou->to/dot_general | solution.py:148
  325.0 4.5 copy.99
  329.6 43.0 %reduce-scatter.2.cloned.1.call-done = bf16[14,1,32,1024]{3,2,0,1:T(8,128)(2,1)} async-done(((bf16[14,4,32,1024]{3,2,0,1:T(8,128)(2,1)}), bf16[14,1,32,1024]{3,2,0,1:T(8,128)(2,1)}) %reduce-scatter.2.cloned.1.call-update) | async-done | bytes 917520 | tf_op jit(solution)/shard_map/reduce_scatter | solution.py:151
  372.6 1.8 fusion.51
  374.4 1.9 multiply_reduce_fusion
  376.4 2.8 add_convert_fusion
  379.2 2.0 gather_fusion.2
  381.3 3.2 broadcast_select_fusion
  384.4 7.8 %all-to-all-start.3 = ((bf16[32,32,1024]{2,1,0:T(8,128)(2,1)}), bf16[32,32,1024]{2,1,0:T(8,128)(2,1)S(1)}, u32[]{:S(2)}, u32[]{:S(2)}) async-start(bf16[32,32,1024]{2,1,0:T(8,128)(2,1)} %broadcast_select_fusion), calls=%async_computation.4 | async-start | bytes 4194304 | tf_op jit(solution)/shard_map/all_to_all | solution.py:163
  392.3 28.5 %all-to-all-done.3 = bf16[32,32,1024]{2,1,0:T(8,128)(2,1)S(1)} async-done(((bf16[32,32,1024]{2,1,0:T(8,128)(2,1)}), bf16[32,32,1024]{2,1,0:T(8,128)(2,1)S(1)}, u32[]{:S(2)}, u32[]{:S(2)}) %all-to-all-start.3) | async-done | bytes 2097184 | tf_op jit(solution)/shard_map/all_to_all | solution.py:163
  420.8 1.5 gather_fusion.3
  422.4 1.3 pad_maximum_fusion
  423.7 3.6 copy.100
  427.3 35.7 %all-gather.17.cloned.1.call-done = bf16[14,128,1024]{2,1,0:T(8,128)(2,1)} async-done(((bf16[14,32,1024]{2,1,0:T(8,128)(2,1)}), bf16[14,128,1024]{2,1,0:T(8,128)(2,1)}) %all-gather.17.cloned.1.call-update) | async-done | bytes 3670032 | tf_op jit(solution)/shard_map/all_gather | solution.py:165
  463.0 4.2 copy.146
  (138 shorter events, 37.9 us)
Async XLA Ops:
  7.9 19.1 %copy-start.18 = (s32[14]{0:T(128)}, s32[14]{0:T(128)S(1)}, u32[]{:S(2)}) copy-start(s32[14]{0:T(128)S(1)} %compare_select_fusion.2) | copy-start | bytes 172
  10.2 16.9 %all-to-all-start = ((s32[32,1,129]{2,1,0:T(1,128)}), s32[32,1,129]{2,1,0:T(1,128)S(1)}, u32[]{:S(2)}, u32[]{:S(2)}) async-start(s32[32,1,129]{2,1,0:T(1,128)} %all_to_all.17), calls=%async_computation | async-start | bytes 65536 | tf_op jit(solution)/shard_map/all_to_all | solution.py:97
  21.1 42.1 %copy-start.12 = (bf16[32,256]{1,0:T(8,128)(2,1)S(1)}, bf16[32,256]{1,0:T(8,128)(2,1)}, u32[]{:S(2)}) copy-start(bf16[32,256]{1,0:T(8,128)(2,1)} %param.26) | copy-start | bytes 49156
  21.1 42.1 %copy-start.13 = (bf16[32,256]{1,0:T(8,128)(2,1)S(1)}, bf16[32,256]{1,0:T(8,128)(2,1)}, u32[]{:S(2)}) copy-start(bf16[32,256]{1,0:T(8,128)(2,1)} %param.27) | copy-start | bytes 49156
  21.1 42.1 %copy-start.14 = (bf16[32,256]{1,0:T(8,128)(2,1)S(1)}, bf16[32,256]{1,0:T(8,128)(2,1)}, u32[]{:S(2)}) copy-start(bf16[32,256]{1,0:T(8,128)(2,1)} %param.28) | copy-start | bytes 49156
  21.1 42.1 %copy-start.10 = (bf16[32,1024]{1,0:T(8,128)(2,1)S(1)}, bf16[32,1024]{1,0:T(8,128)(2,1)}, u32[]{:S(2)}) copy-start(bf16[32,1024]{1,0:T(8,128)(2,1)} %param.30) | copy-start | bytes 196612
  21.1 42.1 %copy-start.15 = (bf16[256,32]{0,1:T(8,128)(2,1)S(1)}, bf16[256,32]{0,1:T(8,128)(2,1)}, u32[]{:S(2)}) copy-start(bf16[256,32]{0,1:T(8,128)(2,1)} %param.29) | copy-start | bytes 49156
  21.1 42.1 %copy-start.11 = (bf16[1024,32]{0,1:T(8,128)(2,1)S(1)}, bf16[1024,32]{0,1:T(8,128)(2,1)}, u32[]{:S(2)}) copy-start(bf16[1024,32]{0,1:T(8,128)(2,1)} %param.31) | copy-start | bytes 196612
  27.1 34.5 %all-to-all-start.1 = ((bf16[32,128,256]{2,1,0:T(8,128)(2,1)}), bf16[32,128,256]{2,1,0:T(8,128)(2,1)S(1)}, u32[]{:S(2)}, u32[]{:S(2)}) async-start(bf16[32,128,256]{2,1,0:T(8,128)(2,1)} %scatter_fusion), calls=%async_computation.1 | async-start | bytes 4194304 | tf_op jit(solution)/shard_map/all_to_all | solution.py:96
  32.9 74.3 %all-gather.13.cloned.1.call-start = ((), (), s32[]{:S(2)}) async-start(), calls=%async_computation.8 | async-start | bytes 4587520 | tf_op jit(solution)/shard_map/all_gather | solution.py:105
  33.6 0.6 copy-start.21
  63.1 98.9 %all-gather.9.cloned.1.call-start = ((), (), s32[]{:S(2)}) async-start(), calls=%async_computation.5 | async-start | bytes 6488064 | tf_op jit(solution)/shard_map/all_gather | solution.py:66
  63.3 0.7 copy-start.7
  64.0 181.7 %all-gather.11.cloned.1.call-start = ((), (), s32[]{:S(2)}) async-start(), calls=%async_computation.6 | async-start | bytes 2621440 | tf_op jit(solution)/shard_map/all_gather | solution.py:79
  165.3 0.9 copy-start
  170.6 1.0 copy-start.2
  195.8 8.1 %copy-start.4 = (bf16[1792,64]{0,1:T(8,128)(2,1)S(1)}, bf16[1792,64]{0,1:T(8,128)(2,1)}, u32[]{:S(2)}) copy-start(bf16[1792,64]{0,1:T(8,128)(2,1)} %get-tuple-element.357) | copy-start | bytes 688132
  195.8 8.4 %copy-start.5 = (bf16[1792,64]{0,1:T(8,128)(2,1)S(1)}, bf16[1792,64]{0,1:T(8,128)(2,1)}, u32[]{:S(2)}) copy-start(bf16[1792,64]{0,1:T(8,128)(2,1)} %get-tuple-element.353) | copy-start | bytes 688132
  195.8 8.7 %copy-start.6 = (bf16[1792,64]{0,1:T(8,128)(2,1)S(1)}, bf16[1792,64]{0,1:T(8,128)(2,1)}, u32[]{:S(2)}) copy-start(bf16[1792,64]{0,1:T(8,128)(2,1)} %get-tuple-element.361) | copy-start | bytes 688132
  206.7 8.0 %copy-start.3 = (bf16[2,896,64]{2,1,0:T(8,128)(2,1)S(1)}, bf16[2,896,64]{2,1,0:T(8,128)(2,1)}, u32[]{:S(2)}) copy-start(bf16[2,896,64]{2,1,0:T(8,128)(2,1)} %copy.82) | copy-start | bytes 688132
  216.3 23.1 %all-to-all-start.2 = ((bf16[14,4,32,256]{3,2,0,1:T(8,128)(2,1)}), bf16[14,4,32,256]{3,2,0,1:T(8,128)(2,1)S(1)}, u32[]{:S(2)}, u32[]{:S(2)}) async-start(bf16[14,4,32,256]{3,2,0,1:T(8,128)(2,1)} %copy.105), calls=%async_computation.2 | async-start | bytes 1835008 | tf_op jit(solution)/shard_map/all_to_all | solution.py:122
  220.2 78.7 %all-gather.15.cloned.1.call-start = ((), (), s32[]{:S(2)}) async-start(), calls=%async_computation.9 | async-start | bytes 4587520 | tf_op jit(solution)/shard_map/all_gather | solution.py:144
  220.2 32.4 %copy-start.8 = (f32[1024]{0:T(1024)S(1)}, f32[1024]{0:T(1024)}, u32[]{:S(2)}) copy-start(f32[1024]{0:T(1024)} %param.33) | copy-start | bytes 12292
  220.2 32.4 %copy-start.9 = (f32[1024]{0:T(1024)S(1)}, f32[1024]{0:T(1024)}, u32[]{:S(2)}) copy-start(f32[1024]{0:T(1024)} %param.32) | copy-start | bytes 12292
  254.0 118.7 %reduce-scatter.2.cloned.1.call-start = ((), (), s32[]{:S(2)}) async-start(), calls=%async_computation.7 | async-start | bytes 4587520 | tf_op jit(solution)/shard_map/reduce_scatter | solution.py:151
  325.0 4.6 copy-start.20
  325.0 4.6 copy-start.22
  329.6 46.8 %copy-start.16 = (f32[1024]{0:T(1024)S(1)}, f32[1024]{0:T(1024)}, u32[]{:S(2)}) copy-start(f32[1024]{0:T(1024)} %param.35) | copy-start | bytes 12292
  329.6 46.8 %copy-start.17 = (f32[1024]{0:T(1024)S(1)}, f32[1024]{0:T(1024)}, u32[]{:S(2)}) copy-start(f32[1024]{0:T(1024)} %param.34) | copy-start | bytes 12292
  379.2 13.0 %copy-start.19 = (s32[14]{0:T(128)S(1)}, s32[14]{0:T(128)}, u32[]{:S(2)}) copy-start(s32[14]{0:T(128)} %copy-done.18) | copy-start | bytes 172
  381.2 41.1 %copy-start.1 = (bf16[1792,256]{0,1:T(8,128)(2,1)S(1)}, bf16[1792,256]{0,1:T(8,128)(2,1)}, u32[]{:S(2)}) copy-start(bf16[1792,256]{0,1:T(8,128)(2,1)} %copy-done) | copy-start | bytes 2752516
  384.4 36.4 %all-to-all-start.3 = ((bf16[32,32,1024]{2,1,0:T(8,128)(2,1)}), bf16[32,32,1024]{2,1,0:T(8,128)(2,1)S(1)}, u32[]{:S(2)}, u32[]{:S(2)}) async-start(bf16[32,32,1024]{2,1,0:T(8,128)(2,1)} %broadcast_select_fusion), calls=%async_computation.4 | async-start | bytes 4194304 | tf_op jit(solution)/shard_map/all_to_all | solution.py:163
  392.2 70.7 %all-gather.17.cloned.1.call-start = ((), (), s32[]{:S(2)}) async-start(), calls=%async_computation.10 | async-start | bytes 4587520 | tf_op jit(solution)/shard_map/all_gather | solution.py:165
Sparse Core Ops, SparseCore 0:
  63.2 43.9 all-gather.12
  110.0 51.8 all-gather.8
  206.8 38.8 all-gather.10
  254.1 44.7 all-gather.14
  329.7 42.8 reduce-scatter.1
  422.5 40.4 all-gather.16
where the time goes:
time: 480 us; the launch traced here: 474 us
  waiting for transfers between devices  304 us (63%)
  matrix products  64.6 us (13%)
  local copies, waits for them, and re-layouts  38.6 us (8%)
  starting transfers between devices  27.4 us (6%)
  other arithmetic  24 us (5%)
  between operations  15 us (3%)
    all_gather x1, waiting for transfers between devices, body(): gathered = lax.all_gather(local, 'dp', axis=0, tiled=True)  54.7 us
    all_gather x1, waiting for transfers between devices, body(): lax.all_gather(first_mine, 'mp', axis=1).reshape(pages_dev * page, width)  44.9 us
    reduce_scatter x1, waiting for transfers between devices, body(): lax.psum_scatter(fed_term.reshape(pages_dev, n_model, sub, width), 'mp',...  43 us
    all_gather x1, waiting for transfers between devices, body(): lax.all_gather(dealt_part, 'mp', axis=2, tiled=True)  42.6 us
    all_gather x1, waiting for transfers between devices, body(): lax.all_gather(mixed_mine, 'mp', axis=1).reshape(pages_dev * page, width)  35.7 us
    all_to_all x1, waiting for transfers between devices, body(): lax.all_to_all(outgoing, 'dp', split_axis=0, concat_axis=0, tiled=True)  28.5 us
    all_to_all x1, waiting for transfers between devices, body(): lax.all_to_all(send_pages, 'dp', split_axis=0, concat_axis=0, tiled=True)  27.3 us
    dot_general x1, matrix products, body(): jnp.einsum('tu,ou->to', hidden, down_t, preferred_element_type=jnp.float32)  26.1 us
  transfers between devices with their start and end apart: 10, of which 10 were waited for; matrix products, arithmetic and copies ran while one was open for 5% of the time, Pallas kernels for 0%

commit v1 on v0

--- a/solution.py
+++ b/solution.py
@@ -4,6 +4,19 @@
 from jax.sharding import PartitionSpec as P
 
 HEAD = 64
+
+
+def ring_gather(x, axis, dim):
+    ways = lax.axis_size(axis)
+    up = [(d, (d + 1) % ways) for d in range(ways)]
+    down = [(d, (d - 1) % ways) for d in range(ways)]
+    earlier, later = ([x], [x])
+    for _ in range(ways // 2):
+        earlier.append(lax.ppermute(earlier[-1], axis, up))
+    for _ in range((ways - 1) // 2):
+        later.append(lax.ppermute(later[-1], axis, down))
+    line = jnp.concatenate([*earlier[::-1], *later[1:]], axis=dim)
+    return jnp.roll(line, (lax.axis_index(axis) - ways // 2) * x.shape[dim], axis=dim)
 
 
 def layer_norm(hidden_sum, gain, shift):
@@ -102,7 +115,7 @@
         jnp.where(matches, jnp.arange(buffer_rows, dtype=jnp.int32)[None, :], 0), axis=1
     )
     dealt_part = got_pages[source_row]
-    dealt = lax.all_gather(dealt_part, "mp", axis=2, tiled=True).reshape(pages_dev * page, width)
+    dealt = ring_gather(dealt_part, "mp", 2).reshape(pages_dev * page, width)
     dealt_ids = got_ids[source_row].reshape(pages_dev * page)
     query = jnp.dot(dealt, full_query, preferred_element_type=jnp.float32).astype(jnp.bfloat16)
     keys = jnp.dot(dealt, full_key, preferred_element_type=jnp.float32).astype(jnp.bfloat16)

time: 480 us -> 451 us (0.940)
  waiting for transfers between devices: 304 us -> 258 us
  local copies, waits for them, and re-layouts: 38.6 us -> 48.5 us
    all_gather x1, waiting for transfers between devices: 54.7 us -> 0.01 us  [body(): gathered = lax.all_gather(local, 'dp', axis=0, tiled=True)]
    all_gather x1 -> x0, waiting for transfers between devices: 42.6 us -> none  [body(): lax.all_gather(dealt_part, 'mp', axis=2, tiled=True)]
    ppermute x0 -> x3, waiting for transfers between devices: none -> 37 us  [the longest x2 37 us: ring_gather(): earlier.append(lax.ppermute(earlier[-1], axis, up))]
    all_to_all x1, waiting for transfers between devices: 27.3 us -> 36.4 us  [body(): lax.all_to_all(send_pages, 'dp', split_axis=0, concat_axis=0, tiled=True)]
    unnamed x54 -> x49, local copies, waits for them, and re-layouts: 11 us -> 17.8 us
    all_gather x1, waiting for transfers between devices: 6.34 us -> 11.6 us  [body(): out_all_t = lax.all_gather(out_t, 'mp', axis=1, tiled=True)]
  transfers between devices with their start and end apart: 10 -> 12, of which waited for: 10 -> 10; matrix products, arithmetic and copies ran while one was open for 5% -> 7% of each run, Pallas kernels for 0% -> 0%
where the time goes in v1:
time: 451 us; the launch traced here: 443 us
  waiting for transfers between devices  258 us (57%)
  matrix products  66.4 us (15%)
  local copies, waits for them, and re-layouts  48.5 us (11%)
  starting transfers between devices  30.9 us (7%)
  other arithmetic  24 us (5%)
  between operations  14.6 us (3%)
    all_gather x1, waiting for transfers between devices, body(): lax.all_gather(first_mine, 'mp', axis=1).reshape(pages_dev * page, width)  43.8 us
    reduce_scatter x1, waiting for transfers between devices, body(): lax.psum_scatter(fed_term.reshape(pages_dev, n_model, sub, width), 'mp',...  43 us
    ppermute x2, waiting for transfers between devices, ring_gather(): earlier.append(lax.ppermute(earlier[-1], axis, up))  37 us
    all_to_all x1, waiting for transfers between devices, body(): lax.all_to_all(send_pages, 'dp', split_axis=0, concat_axis=0, tiled=True)  36.4 us
    all_gather x1, waiting for transfers between devices, body(): lax.all_gather(mixed_mine, 'mp', axis=1).reshape(pages_dev * page, width)  35.7 us
    all_to_all x1, waiting for transfers between devices, body(): lax.all_to_all(outgoing, 'dp', split_axis=0, concat_axis=0, tiled=True)  28.5 us
    dot_general x1, matrix products, body(): jnp.einsum('tu,ou->to', hidden, down_t, preferred_element_type=jnp.float32)  26.1 us
    all_to_all x1, waiting for transfers between devices, body(): lax.all_to_all(context.reshape(pages_dev, n_model, sub, head_cols), 'mp',...  20.2 us
  transfers between devices with their start and end apart: 12, of which 10 were waited for; matrix products, arithmetic and copies ran while one was open for 7% of the time, Pallas kernels for 0%

profile of v1, /device:TPU:1, one launch (start us, length us, event | category | flops | bytes accessed | tf_op | source)
XLA Modules:
  0.0 443.2 jit_solution(5221886848913191905)
XLA Ops:
  15.5 9.6 %all-to-all-start = ((s32[32,1,129]{2,1,0:T(1,128)}), s32[32,1,129]{2,1,0:T(1,128)S(1)}, u32[]{:S(2)}, u32[]{:S(2)}) async-start(s32[32,1,129]{2,1,0:T(1,128)} %all_to_all.17), calls=%async_computation | async-start | bytes 65536 | tf_op jit(solution)/shard_map/all_to_all | solution.py:110
  26.4 1.6 broadcast_in_dim.96
  28.0 2.8 scatter_fusion
  30.8 1.6 all-to-all-done
  32.4 5.8 %all-to-all-start.1 = ((bf16[32,128,256]{2,1,0:T(8,128)(2,1)}), bf16[32,128,256]{2,1,0:T(8,128)(2,1)S(1)}, u32[]{:S(2)}, u32[]{:S(2)}) async-start(bf16[32,128,256]{2,1,0:T(8,128)(2,1)} %scatter_fusion), calls=%async_computation.1 | async-start | bytes 4194304 | tf_op jit(solution)/shard_map/all_to_all | solution.py:109
  39.5 36.4 %all-to-all-done.1 = bf16[32,128,256]{2,1,0:T(8,128)(2,1)S(1)} async-done(((bf16[32,128,256]{2,1,0:T(8,128)(2,1)}), bf16[32,128,256]{2,1,0:T(8,128)(2,1)S(1)}, u32[]{:S(2)}, u32[]{:S(2)}) %all-to-all-start.1) | async-done | bytes 2097184 | tf_op jit(solution)/shard_map/all_to_all | solution.py:109
  77.8 19.9 %collective-permute-done = bf16[14,128,256]{2,1,0:T(8,128)(2,1)S(1)} collective-permute-done((bf16[14,128,256]{2,1,0:T(8,128)(2,1)S(1)}, bf16[14,128,256]{2,1,0:T(8,128)(2,1)S(1)}, u32[]{:S(2)}, u32[]{:S(2)}) %collective-permute-start) | collective-permute-done | bytes 917536 | tf_op jit(solution)/shard_map/ppermute | solution.py:15
  97.7 2.6 collective-permute-start.2
  101.0 17.1 %collective-permute-done.1 = bf16[14,128,256]{2,1,0:T(8,128)(2,1)} collective-permute-done((bf16[14,128,256]{2,1,0:T(8,128)(2,1)S(1)}, bf16[14,128,256]{2,1,0:T(8,128)(2,1)}, u32[]{:S(2)}, u32[]{:S(2)}) %collective-permute-start.1) | collective-permute-done | bytes 917536 | tf_op jit(solution)/shard_map/ppermute | solution.py:15
  121.5 2.3 constant_dynamic-slice_fusion
  123.7 3.3 convolution_convert_fusion.2
  129.0 3.3 convolution_convert_fusion.1
  134.3 3.3 convolution_convert_fusion.3
  138.6 8.2 %while.41 = (s32[]{:T(128)}, bf16[2,896,64]{1,2,0:T(8,128)(2,1)S(1)}, s32[2,896]{1,0:T(2,128)S(1)}, s32[14,128]{1,0:T(8,128)S(1)}, bf16[2,896,64]{2,1,0:T(8,128)...) while((s32[]{:T(128)}, bf16[2,896,64]{1,2,0:T(8,128)(2,1)S(1)}, ...), condition=%wide.region_7.8_spmd, body=%wide.region_4.7_spmd.sunk | while | flops 425548032 | bytes 20567648 | solution.py:46
  141.5 1.5 fusion.137
  145.3 1.5 fusion.137
  148.7 7.6 %while.42 = (s32[]{:T(128)}, bf16[2,896,64]{1,2,0:T(8,128)(2,1)S(1)}, s32[2,896]{1,0:T(2,128)S(1)}, s32[14,128]{1,0:T(8,128)S(1)}, bf16[2,896,64]{2,1,0:T(8,128)...) while((s32[]{:T(128)}, bf16[2,896,64]{1,2,0:T(8,128)(2,1)S(1)}, ...), condition=%wide.region_11.12_spmd, body=%wide.region_8.11_spmd.sunk | while | flops 425548032 | bytes 20567648 | solution.py:46
  151.0 1.5 fusion.142
  154.8 1.5 fusion.142
  157.5 7.8 %while.43 = (s32[]{:T(128)}, bf16[2,896,64]{1,2,0:T(8,128)(2,1)S(1)}, s32[2,896]{1,0:T(2,128)S(1)}, s32[14,128]{1,0:T(8,128)S(1)}, bf16[2,896,64]{2,1,0:T(8,128)...) while((s32[]{:T(128)}, bf16[2,896,64]{1,2,0:T(8,128)(2,1)S(1)}, ...), condition=%wide.region_15.16_spmd, body=%wide.region_12.15_spmd.sunk | while | flops 425548032 | bytes 20567648 | solution.py:46
  159.8 1.5 fusion.147
  163.6 1.5 fusion.147
  167.2 1.9 slice.152
  169.1 9.6 %while.44 = (s32[]{:T(128)}, bf16[2,896,64]{1,2,0:T(8,128)(2,1)S(1)}, s32[2,896]{1,0:T(2,128)S(1)}, s32[14,128]{1,0:T(8,128)S(1)}, bf16[2,896,64]{2,1,0:T(8,128)...) while((s32[]{:T(128)}, bf16[2,896,64]{1,2,0:T(8,128)(2,1)S(1)}, ...), condition=%wide.region_19.20_spmd, body=%wide.region_16.19_spmd.sunk | while | flops 425548032 | bytes 20337244 | solution.py:46
  169.2 2.2 fusion.150
  172.4 1.5 fusion.152
  174.0 2.2 fusion.150
  177.2 1.5 fusion.152
  180.6 3.5 all-to-all-start.2
  184.2 20.2 %all-to-all-done.2 = bf16[14,4,32,256]{3,2,0,1:T(8,128)(2,1)S(1)} async-done(((bf16[14,4,32,256]{3,2,0,1:T(8,128)(2,1)}), bf16[14,4,32,256]{3,2,0,1:T(8,128)(2,1)S(1)}, u32[]{:S(2)}, u32[]{:S(2)}) %all-to-all-start.2) | async-done | bytes 917536 | tf_op jit(solution)/shard_map/all_to_all | solution.py:135
  204.4 11.6 %all-gather.9.cloned.1.call-done = bf16[1024,1024]{1,0:T(8,128)(2,1)} async-done(((bf16[1024,256]{1,0:T(8,128)(2,1)}), bf16[1024,1024]{1,0:T(8,128)(2,1)}) %all-gather.9.cloned.1.call-update) | async-done | bytes 2097168 | tf_op jit(solution)/shard_map/all_gather | solution.py:92
  218.9 1.5 convolution_convert_fusion.5
  220.4 2.2 fusion.100
  224.3 43.8 %all-gather.11.cloned.1.call-done = bf16[14,128,1024]{2,1,0:T(8,128)(2,1)} async-done(((bf16[14,32,1024]{2,1,0:T(8,128)(2,1)}), bf16[14,128,1024]{2,1,0:T(8,128)(2,1)}) %all-gather.11.cloned.1.call-update) | async-done | bytes 3670032 | tf_op jit(solution)/shard_map/all_gather | solution.py:157
  268.1 26.1 %convolution_convert_fusion = bf16[1792,1024]{1,0:T(8,128)(2,1)} fusion(bf16[1024,3072]{1,0:T(8,128)(2,1)} %all-gather.7.cloned.1.call-done, bf16[1792,1024]{1,0:T(8,128)(2,1)} %bitcast.186), kind=kOutput, calls=%fused_computation.73 | convolution fusion | flops 7637303296 | bytes 11534336 | tf_op jit(solution)/shard_map/tu,ou->to/dot_general | solution.py:161
  294.3 4.5 %copy.99 = bf16[14,4,32,1024]{3,2,0,1:T(8,128)(2,1)} copy(bf16[14,4,32,1024]{3,2,1,0:T(8,128)(2,1)} %bitcast.169) | data formatting | bytes 7340032 | tf_op jit(solution)/shard_map/reshape | solution.py:165
  298.8 43.0 %reduce-scatter.2.cloned.1.call-done = bf16[14,1,32,1024]{3,2,0,1:T(8,128)(2,1)} async-done(((bf16[14,4,32,1024]{3,2,0,1:T(8,128)(2,1)}), bf16[14,1,32,1024]{3,2,0,1:T(8,128)(2,1)}) %reduce-scatter.2.cloned.1.call-update) | async-done | bytes 917520 | tf_op jit(solution)/shard_map/reduce_scatter | solution.py:164
  341.8 1.8 fusion.51
  343.7 1.9 multiply_reduce_fusion
  345.6 2.8 add_convert_fusion
  348.5 2.0 gather_fusion.2
  350.5 3.2 broadcast_select_fusion
  353.7 7.8 %all-to-all-start.3 = ((bf16[32,32,1024]{2,1,0:T(8,128)(2,1)}), bf16[32,32,1024]{2,1,0:T(8,128)(2,1)S(1)}, u32[]{:S(2)}, u32[]{:S(2)}) async-start(bf16[32,32,1024]{2,1,0:T(8,128)(2,1)} %broadcast_select_fusion), calls=%async_computation.4 | async-start | bytes 4194304 | tf_op jit(solution)/shard_map/all_to_all | solution.py:176
  361.5 28.5 %all-to-all-done.3 = bf16[32,32,1024]{2,1,0:T(8,128)(2,1)S(1)} async-done(((bf16[32,32,1024]{2,1,0:T(8,128)(2,1)}), bf16[32,32,1024]{2,1,0:T(8,128)(2,1)S(1)}, u32[]{:S(2)}, u32[]{:S(2)}) %all-to-all-start.3) | async-done | bytes 2097184 | tf_op jit(solution)/shard_map/all_to_all | solution.py:176
  390.0 1.5 gather_fusion.3
  393.0 3.6 copy.100
  396.5 35.7 %all-gather.13.cloned.1.call-done = bf16[14,128,1024]{2,1,0:T(8,128)(2,1)} async-done(((bf16[14,32,1024]{2,1,0:T(8,128)(2,1)}), bf16[14,128,1024]{2,1,0:T(8,128)(2,1)}) %all-gather.13.cloned.1.call-update) | async-done | bytes 3670032 | tf_op jit(solution)/shard_map/all_gather | solution.py:178
  432.2 4.2 copy.153
  (138 shorter events, 50.2 us)
Async XLA Ops:
  7.2 116.6 %all-gather.7.cloned.1.call-start = ((), (), s32[]{:S(2)}) async-start(), calls=%async_computation.5 | async-start | bytes 6488064 | tf_op jit(solution)/shard_map/all_gather | solution.py:79
  11.8 0.7 copy-start.7
  13.3 19.0 %copy-start.12 = (s32[14]{0:T(128)}, s32[14]{0:T(128)S(1)}, u32[]{:S(2)}) copy-start(s32[14]{0:T(128)S(1)} %compare_select_fusion.2) | copy-start | bytes 172
  15.5 16.9 %all-to-all-start = ((s32[32,1,129]{2,1,0:T(1,128)}), s32[32,1,129]{2,1,0:T(1,128)S(1)}, u32[]{:S(2)}, u32[]{:S(2)}) async-start(s32[32,1,129]{2,1,0:T(1,128)} %all_to_all.17), calls=%async_computation | async-start | bytes 65536 | tf_op jit(solution)/shard_map/all_to_all | solution.py:110
  32.4 43.5 %all-to-all-start.1 = ((bf16[32,128,256]{2,1,0:T(8,128)(2,1)}), bf16[32,128,256]{2,1,0:T(8,128)(2,1)S(1)}, u32[]{:S(2)}, u32[]{:S(2)}) async-start(bf16[32,128,256]{2,1,0:T(8,128)(2,1)} %scatter_fusion), calls=%async_computation.1 | async-start | bytes 4194304 | tf_op jit(solution)/shard_map/all_to_all | solution.py:109
  38.2 177.8 %all-gather.9.cloned.1.call-start = ((), (), s32[]{:S(2)}) async-start(), calls=%async_computation.6 | async-start | bytes 2621440 | tf_op jit(solution)/shard_map/all_gather | solution.py:92
  38.9 0.5 copy-start.15
  76.5 21.2 %collective-permute-start = (bf16[14,128,256]{2,1,0:T(8,128)(2,1)S(1)}, bf16[14,128,256]{2,1,0:T(8,128)(2,1)S(1)}, u32[]{:S(2)}, u32[]{:S(2)}) collective-permute-start(bf16[14,128,256]{2,1,0:T(8,128)(2,1)S(1)} %gather_fusion), channel_id=1, source_target_pairs={{0,1},{1,2},{2,3},{3,0},{4,5},{5,6},{6,7},{7,4},{8,9},{9,10},{10,1... | collective-permute-start | bytes 2752520 | tf_op jit(solution)/shard_map/ppermute | solution.py:15
  97.7 20.4 %collective-permute-start.1 = (bf16[14,128,256]{2,1,0:T(8,128)(2,1)S(1)}, bf16[14,128,256]{2,1,0:T(8,128)(2,1)}, u32[]{:S(2)}, u32[]{:S(2)}) collective-permute-start(bf16[14,128,256]{2,1,0:T(8,128)(2,1)S(1)} %collective-permute-done), channel_id=1, source_target_pairs={{0,1},{1,2},{2,3},{3,0},{4,5},{5,6},{6,7},{7,4},{8,9},{9,10},{10,1... | collective-permute-start | bytes 2752520 | tf_op jit(solution)/shard_map/ppermute | solution.py:15
  97.7 21.9 %collective-permute-start.2 = (bf16[14,128,256]{2,1,0:T(8,128)(2,1)S(1)}, bf16[14,128,256]{2,1,0:T(8,128)(2,1)S(1)}, u32[]{:S(2)}, u32[]{:S(2)}) collective-permute-start(bf16[14,128,256]{2,1,0:T(8,128)(2,1)S(1)} %gather_fusion), channel_id=1, source_target_pairs={{0,3},{1,0},{2,1},{3,2},{4,7},{5,4},{6,5},{7,6},{8,11},{9,8},{10,9... | collective-permute-start | bytes 2752520 | tf_op jit(solution)/shard_map/ppermute | solution.py:17
  127.0 1.0 copy-start
  132.3 0.9 copy-start.2
  157.5 8.1 %copy-start.4 = (bf16[1792,64]{0,1:T(8,128)(2,1)S(1)}, bf16[1792,64]{0,1:T(8,128)(2,1)}, u32[]{:S(2)}) copy-start(bf16[1792,64]{0,1:T(8,128)(2,1)} %get-tuple-element.357) | copy-start | bytes 688132
  157.5 8.4 %copy-start.5 = (bf16[1792,64]{0,1:T(8,128)(2,1)S(1)}, bf16[1792,64]{0,1:T(8,128)(2,1)}, u32[]{:S(2)}) copy-start(bf16[1792,64]{0,1:T(8,128)(2,1)} %get-tuple-element.353) | copy-start | bytes 688132
  157.5 8.7 %copy-start.6 = (bf16[1792,64]{0,1:T(8,128)(2,1)S(1)}, bf16[1792,64]{0,1:T(8,128)(2,1)}, u32[]{:S(2)}) copy-start(bf16[1792,64]{0,1:T(8,128)(2,1)} %get-tuple-element.361) | copy-start | bytes 688132
  169.1 9.9 %copy-start.3 = (bf16[2,896,64]{2,1,0:T(8,128)(2,1)S(1)}, bf16[2,896,64]{2,1,0:T(8,128)(2,1)}, u32[]{:S(2)}) copy-start(bf16[2,896,64]{2,1,0:T(8,128)(2,1)} %copy.82) | copy-start | bytes 688132
  180.6 23.8 %all-to-all-start.2 = ((bf16[14,4,32,256]{3,2,0,1:T(8,128)(2,1)}), bf16[14,4,32,256]{3,2,0,1:T(8,128)(2,1)S(1)}, u32[]{:S(2)}, u32[]{:S(2)}) async-start(bf16[14,4,32,256]{3,2,0,1:T(8,128)(2,1)} %copy.105), calls=%async_computation.2 | async-start | bytes 1835008 | tf_op jit(solution)/shard_map/all_to_all | solution.py:135
  184.1 84.0 %all-gather.11.cloned.1.call-start = ((), (), s32[]{:S(2)}) async-start(), calls=%async_computation.8 | async-start | bytes 4587520 | tf_op jit(solution)/shard_map/all_gather | solution.py:157
  184.2 38.7 %copy-start.8 = (f32[1024]{0:T(1024)S(1)}, f32[1024]{0:T(1024)}, u32[]{:S(2)}) copy-start(f32[1024]{0:T(1024)} %param.33) | copy-start | bytes 12292
  184.2 38.7 %copy-start.9 = (f32[1024]{0:T(1024)S(1)}, f32[1024]{0:T(1024)}, u32[]{:S(2)}) copy-start(f32[1024]{0:T(1024)} %param.32) | copy-start | bytes 12292
  224.2 117.6 %reduce-scatter.2.cloned.1.call-start = ((), (), s32[]{:S(2)}) async-start(), calls=%async_computation.7 | async-start | bytes 4587520 | tf_op jit(solution)/shard_map/reduce_scatter | solution.py:164
  294.2 4.6 %copy-start.14 = (s32[32]{0:T(128)S(1)}, s32[32]{0:T(128)}, u32[]{:S(2)}) copy-start(s32[32]{0:T(128)} %get-tuple-element.286) | copy-start | bytes 388
  294.2 4.6 %copy-start.16 = (s32[32]{0:T(128)S(1)}, s32[32]{0:T(128)}, u32[]{:S(2)}) copy-start(s32[32]{0:T(128)} %copy-done.15) | copy-start | bytes 388
  298.8 46.8 %copy-start.10 = (f32[1024]{0:T(1024)S(1)}, f32[1024]{0:T(1024)}, u32[]{:S(2)}) copy-start(f32[1024]{0:T(1024)} %param.35) | copy-start | bytes 12292
  298.8 46.8 %copy-start.11 = (f32[1024]{0:T(1024)S(1)}, f32[1024]{0:T(1024)}, u32[]{:S(2)}) copy-start(f32[1024]{0:T(1024)} %param.34) | copy-start | bytes 12292
  348.4 13.1 %copy-start.13 = (s32[14]{0:T(128)S(1)}, s32[14]{0:T(128)}, u32[]{:S(2)}) copy-start(s32[14]{0:T(128)} %copy-done.12) | copy-start | bytes 172
  350.5 41.1 %copy-start.1 = (bf16[1792,256]{0,1:T(8,128)(2,1)S(1)}, bf16[1792,256]{0,1:T(8,128)(2,1)}, u32[]{:S(2)}) copy-start(bf16[1792,256]{0,1:T(8,128)(2,1)} %copy-done) | copy-start | bytes 2752516
  353.7 36.4 %all-to-all-start.3 = ((bf16[32,32,1024]{2,1,0:T(8,128)(2,1)}), bf16[32,32,1024]{2,1,0:T(8,128)(2,1)S(1)}, u32[]{:S(2)}, u32[]{:S(2)}) async-start(bf16[32,32,1024]{2,1,0:T(8,128)(2,1)} %broadcast_select_fusion), calls=%async_computation.4 | async-start | bytes 4194304 | tf_op jit(solution)/shard_map/all_to_all | solution.py:176
  361.4 70.7 %all-gather.13.cloned.1.call-start = ((), (), s32[]{:S(2)}) async-start(), calls=%async_computation.9 | async-start | bytes 4587520 | tf_op jit(solution)/shard_map/all_gather | solution.py:178
Sparse Core Ops, SparseCore 0:
  12.6 66.4 all-gather.6
  169.2 46.6 all-gather.8
  224.4 43.7 all-gather.10
  298.9 42.8 reduce-scatter.1
  391.7 40.4 all-gather.12
